TPU v7x, 512 devices: a whole 4x4x16 slice. The times are simulated.
512 devices in a mesh: row: 16 (over z), col: 32 (over x, y, core).
Axes of the slice: x: 4, y: 4, z: 16, core: 2. Of those that a mesh axis runs over, the one named last changes fastest.
Arguments:
- feats: bfloat16 [8192, 4096], P('row', 'col'), may hold values from -6 to 6
- prior_factor: bfloat16 [8192, 2048], P('row', 'col'), may hold values from -0.02 to 0.02, as said below
- ridge: float32 [1024], P('col'), may hold values from 0.5 to 2
Outputs:
- factor: float32 [8192, 1024], P('row', 'col')
Inputs may be any that keep to these rules, and one draw needn't show every extreme that they name: `prior_factor`: entries are independent.
All inputs are finite; a program needn't handle non-finite values.
Results may differ from a plain program's by a relative error of at most 0.0003.
Values may be sent and summed in bfloat16 or wider, within the bound.
No kernel may reach another device: no remote copies, remote signals or barrier semaphores. Data moves between devices by JAX's collectives and lax.ppermute only.
A program may use at most 128 MiB of HBM per device.

v0:
```python
import jax
import jax.numpy as jnp
from jax import lax
from jax.sharding import PartitionSpec as P

EDGES = 4096
PANEL = 512


def in_one_piece(arrays, axis, dim, along):
    widths = [a.shape[along] for a in arrays]
    both = jnp.concatenate(arrays, axis=along)
    whole = lax.all_gather(both, axis, axis=dim, tiled=True)
    return tuple(jnp.split(whole, [sum(widths[:k]) for k in range(1, len(widths))], axis=along))


def copy_for_each(x, axis):
    count = lax.axis_size(axis)
    return lax.all_to_all(jnp.broadcast_to(x[None], (count, *x.shape)), axis, 0, 0, tiled=True)


def of_everyone(x, axis):
    return copy_for_each(x, axis).sum(axis=0)


def together(arrays, axis):
    ends = [0]
    for a in arrays:
        ends.append(ends[-1] + a.size)
    subtotal = of_everyone(jnp.concatenate([a.ravel() for a in arrays]), axis)
    return tuple((subtotal[b:e].reshape(a.shape) for a, b, e in zip(arrays, ends, ends[1:])))


def in_one_piece_2(arrays, axis, dim, along):
    both = jnp.concatenate(arrays, axis=along)
    whole, at, gathered = (lax.psum_scatter(both, axis, scatter_dimension=dim, tiled=True), 0, [])
    for a in arrays:
        gathered.append(lax.slice_in_dim(whole, at, at + a.shape[along], axis=along))
        at += a.shape[along]
    return tuple(gathered)


def joined_along(tiles, dim):
    dims = list(tiles.shape[1:])
    dims[dim] *= tiles.shape[0]
    return jnp.moveaxis(tiles, 0, dim).reshape(dims)


def gather_directly(x, axis, dim):
    tiles = copy_for_each(x, axis)
    return joined_along(tiles, dim)


def subject_rows(parts, groups, count):
    width = parts.shape[-1]
    return parts.reshape(groups, count, width).transpose(1, 0, 2).reshape(groups * count, width)


def panel_cholesky(block, panel):
    top = jnp.linalg.cholesky(block[:panel, :panel])
    lower_left = jax.scipy.linalg.solve_triangular(top, block[panel:, :panel].T, lower=True).T
    rest = block[panel:, panel:] - jnp.dot(
        lower_left, lower_left.T, precision=lax.Precision.HIGHEST
    )
    bottom = jnp.linalg.cholesky(rest)
    upper = jnp.concatenate([top, jnp.zeros((panel, block.shape[0] - panel), jnp.float32)], axis=1)
    lower = jnp.concatenate([lower_left, bottom], axis=1)
    return jnp.concatenate([upper, lower], axis=0)


def body(feats, prior_factor, ridge):
    groups = lax.axis_size("row")
    lanes = lax.axis_size("col")
    row_pos = lax.axis_index("row")
    col_pos = lax.axis_index("col")
    rows_here = feats.shape[0]
    cols_here = ridge.shape[0]
    total_cols = cols_here * lanes
    leading = total_cols // groups
    col_feats, col_prior = in_one_piece((feats[:leading], prior_factor[:leading]), "row", 0, 1)
    col_feats = subject_rows(col_feats, groups, leading)
    col_prior = subject_rows(col_prior, groups, leading)
    gram_part = jnp.dot(feats, col_feats.T, preferred_element_type=jnp.float32)
    update_part = jnp.dot(prior_factor, col_prior.T, preferred_element_type=jnp.float32)
    wide_feats = feats.astype(jnp.float32)
    wide_cols = col_feats.astype(jnp.float32)
    row_sq, col_sq = together(
        (jnp.sum(wide_feats * wide_feats, axis=1), jnp.sum(wide_cols * wide_cols, axis=1)), "col"
    )
    gram, update = in_one_piece_2((gram_part, update_part), "col", 1, 0)
    col_start = col_pos * cols_here
    own_sq = lax.dynamic_slice_in_dim(col_sq, col_start, cols_here)
    kernel = jnp.exp(-(row_sq[:, None] + own_sq[None, :] - 2.0 * gram) / EDGES)
    subject = lax.broadcasted_iota(jnp.int32, (rows_here, cols_here), 0) * groups + row_pos
    column = lax.broadcasted_iota(jnp.int32, (rows_here, cols_here), 1) + col_start
    system = kernel + jnp.where(subject == column, ridge[None, :], jnp.zeros_like(kernel)) - update
    head = system[:leading]
    by_rows = gather_directly(head, "row", 0)
    by_cols = lax.all_gather(by_rows, "col", axis=1, tiled=True)
    square = subject_rows(by_cols, groups, leading)
    diag_factor = panel_cholesky(square, PANEL)
    wide_rows = gather_directly(system, "col", 1)
    solved = jax.scipy.linalg.solve_triangular(diag_factor, wide_rows.T, lower=True).T
    factor = lax.dynamic_slice_in_dim(solved, col_start, cols_here, 1)
    return factor


def solution(mesh):
    return jax.shard_map(
        body,
        mesh=mesh,
        in_specs=(P("row", "col"), P("row", "col"), P("col")),
        out_specs=P("row", "col"),
        check_vma=False,
    )
```

profile of v0, /device:TPU:1, one launch (start us, length us, event | category | flops | bytes accessed | tf_op | source)
XLA Modules:
  0.0 660.8 jit_solution(11873660757223299624)
XLA Ops:
  8.1 31.8 %all_gather.6 = bf16[1024,192]{1,0:T(8,128)(2,1)S(1)} all-gather(bf16[64,192]{1,0:T(8,128)(2,1)S(1)} %pad_maximum_fusion.3), channel_id=1, replica_groups=mesh['row'=16,'col'=32] {'row'}, dimensions={0}, use_global_device_ids=true | all-gather | bytes 417792 | tf_op jit(solution)/shard_map/all_gather | solution.py:13
  50.5 15.3 %all-to-all-start = ((f32[32,1,1536]{2,1,0:T(1,128)}), f32[32,1,1536]{2,1,0:T(1,128)S(1)}, u32[]{:S(2)}, u32[]{:S(2)}) async-start(f32[32,1,1536]{2,1,0:T(1,128)} %broadcast_in_dim.18), calls=%async_computation | async-start | bytes 393216 | tf_op jit(solution)/shard_map/all_to_all | solution.py:19
  74.3 81.9 %reduce-scatter.4.cloned.1.call-done = f32[32,1024]{1,0:T(8,128)} async-done(((f32[1024,1024]{1,0:T(8,128)}), f32[32,1024]{1,0:T(8,128)}) %reduce-scatter.4.cloned.1.call-update) | async-done | bytes 131088
  157.4 23.8 %all_to_all.16 = f32[16,1,2048]{2,1,0:T(1,128)S(1)} all-to-all(f32[16,1,2048]{2,1,0:T(1,128)S(1)} %reshape.143), channel_id=1, replica_groups=mesh['row'=16,'col'=32] {'row'}, dimensions={0} | all-to-all | bytes 262144 | tf_op jit(solution)/shard_map/all_to_all | solution.py:19
  185.5 8.8 %all-to-all-start.2 = ((f32[32,512,32]{1,2,0:T(8,128)}), f32[32,512,32]{1,2,0:T(8,128)S(1)}, u32[]{:S(2)}, u32[]{:S(2)}) async-start(f32[32,512,32]{1,2,0:T(8,128)} %broadcast_in_dim.24), calls=%async_computation.2 | async-start | bytes 4194304 | tf_op jit(solution)/shard_map/all_to_all | solution.py:19
  194.3 53.5 %all-gather.2.cloned.1.call-done = f32[1024,1024]{0,1:T(8,128)} async-done(((f32[1024,32]{0,1:T(8,128)}), f32[1024,1024]{0,1:T(8,128)}) %all-gather.2.cloned.1.call-update) | async-done | bytes 4194320 | tf_op jit(solution)/shard_map/all_gather | solution.py:99
  267.5 11.7 %cholesky.286 = f32[128,128]{1,0:T(8,128)S(1)} custom-call(f32[128,128]{1,0:T(8,128)S(1)} %cholesky.426), custom_call_target="Cholesky" | custom-call | tf_op jit(solution)/shard_map/jit(cholesky)/cholesky | solution.py:60
  282.0 9.8 %custom-call.33 = f32[1,128,128]{1,2,0:T(8,128)S(1)} custom-call(f32[1,128,128]{2,1,0:T(8,128)S(1)} %get-tuple-element.91), custom_call_target="InvertDiagBlocksLowerTriangular" | custom-call | tf_op jit(solution)/shard_map/jit(cholesky)/cholesky | solution.py:60
  294.3 11.9 %cholesky.305 = f32[128,128]{1,0:T(8,128)S(1)} custom-call(f32[128,128]{1,0:T(8,128)S(1)} %cholesky.430), custom_call_target="Cholesky" | custom-call | tf_op jit(solution)/shard_map/jit(cholesky)/cholesky | solution.py:60
  306.2 9.8 %custom-call.34 = f32[1,128,128]{1,2,0:T(8,128)S(1)} custom-call(f32[1,128,128]{2,1,0:T(8,128)S(1)} %get-tuple-element.88), custom_call_target="InvertDiagBlocksLowerTriangular" | custom-call | tf_op jit(solution)/shard_map/jit(cholesky)/cholesky | solution.py:60
  317.6 11.7 %cholesky.326 = f32[128,128]{1,0:T(8,128)S(1)} custom-call(f32[128,128]{1,0:T(8,128)S(1)} %cholesky.435), custom_call_target="Cholesky" | custom-call | tf_op jit(solution)/shard_map/jit(cholesky)/cholesky | solution.py:60
  330.0 9.8 %custom-call.35 = f32[1,128,128]{1,2,0:T(8,128)S(1)} custom-call(f32[1,128,128]{2,1,0:T(8,128)S(1)} %get-tuple-element.85), custom_call_target="InvertDiagBlocksLowerTriangular" | custom-call | tf_op jit(solution)/shard_map/jit(cholesky)/cholesky | solution.py:60
  341.3 12.1 %cholesky.343 = f32[128,128]{1,0:T(8,128)S(1)} custom-call(f32[128,128]{1,0:T(8,128)S(1)} %convolution_subtract_fusion.16), custom_call_target="Cholesky" | custom-call | tf_op jit(solution)/shard_map/jit(cholesky)/cholesky | solution.py:60
  358.9 13.6 %while.2 = (s32[]{:T(128)}, f32[512,512]{1,0:T(8,128)}, s32[4,2]{0,1:T(2,128)S(1)}, f32[4,128,128]{2,1,0:T(8,128)}, s32[]{:T(128)}) while((s32[]{:T(128)}, f32[512,512]{1,0:T(8,128)}, s32[4,2]{0,1:T(2,128)S(1)}, f32[4,128,128]{2,1,0:T(8,128)}, s32[]{:T(128)}) %tuple.73), condition=%wide.while_cond, body=%wide.while_body.sunk | while | flops 2 | bytes 132205 | solution.py:61
  372.4 40.1 %custom-call.28 = f32[4,128,128]{1,2,0:T(8,128)S(1)} custom-call(f32[4,128,128]{2,1,0:T(8,128)} %get-tuple-element.13), custom_call_target="InvertDiagBlocksLowerTriangular" | custom-call | tf_op jit(solution)/shard_map/jit(_solve_triangular)/triangular_solve | solution.py:61
  434.4 11.7 %cholesky.358 = f32[128,128]{1,0:T(8,128)S(1)} custom-call(f32[128,128]{1,0:T(8,128)S(1)} %cholesky.439), custom_call_target="Cholesky" | custom-call | tf_op jit(solution)/shard_map/jit(cholesky)/cholesky | solution.py:65
  446.7 9.8 %custom-call.36 = f32[1,128,128]{1,2,0:T(8,128)S(1)} custom-call(f32[1,128,128]{2,1,0:T(8,128)S(1)} %get-tuple-element.81), custom_call_target="InvertDiagBlocksLowerTriangular" | custom-call | tf_op jit(solution)/shard_map/jit(cholesky)/cholesky | solution.py:65
  461.8 13.2 %cholesky.377 = f32[128,128]{1,0:T(8,128)} custom-call(f32[128,128]{1,0:T(8,128)} %cholesky.443), custom_call_target="Cholesky" | custom-call | tf_op jit(solution)/shard_map/jit(cholesky)/cholesky | solution.py:65
  476.5 9.8 %custom-call.37 = f32[1,128,128]{1,2,0:T(8,128)S(1)} custom-call(f32[1,128,128]{2,1,0:T(8,128)S(1)} %get-tuple-element.78), custom_call_target="InvertDiagBlocksLowerTriangular" | custom-call | tf_op jit(solution)/shard_map/jit(cholesky)/cholesky | solution.py:65
  487.9 11.7 %cholesky.398 = f32[128,128]{1,0:T(8,128)S(1)} custom-call(f32[128,128]{1,0:T(8,128)S(1)} %cholesky.448), custom_call_target="Cholesky" | custom-call | tf_op jit(solution)/shard_map/jit(cholesky)/cholesky | solution.py:65
  500.3 10.0 %custom-call.38 = f32[1,128,128]{1,2,0:T(8,128)S(1)} custom-call(f32[1,128,128]{2,1,0:T(8,128)S(1)} %get-tuple-element.75), custom_call_target="InvertDiagBlocksLowerTriangular" | custom-call | tf_op jit(solution)/shard_map/jit(cholesky)/cholesky | solution.py:65
  511.8 11.7 %cholesky.415 = f32[128,128]{1,0:T(8,128)S(1)} custom-call(f32[128,128]{1,0:T(8,128)S(1)} %convolution_subtract_fusion.15), custom_call_target="Cholesky" | custom-call | tf_op jit(solution)/shard_map/jit(cholesky)/cholesky | solution.py:65
  530.6 27.2 %while.3 = (s32[]{:T(128)}, f32[1024,1024]{1,0:T(8,128)}, s32[8,2]{0,1:T(2,128)S(1)}, f32[8,128,128]{2,1,0:T(8,128)}, s32[]{:T(128)}) while((s32[]{:T(128)}, f32[1024,1024]{1,0:T(8,128)}, s32[8,2]{0,1:T(2,128)S(1)}, f32[8,128,128]{2,1,0:T(8,128)}, s32[]{:T(128)}) %tuple.76), condition=%wide.while_cond.1, body=%wide.while_body.1.sunk | while | flops 2 | bytes 132205 | solution.py:103
  557.8 79.6 %custom-call.29 = f32[8,128,128]{1,2,0:T(8,128)S(1)} custom-call(f32[8,128,128]{2,1,0:T(8,128)} %get-tuple-element.21), custom_call_target="InvertDiagBlocksLowerTriangular" | custom-call | tf_op jit(solution)/shard_map/jit(_solve_triangular)/triangular_solve | solution.py:103
  (187 shorter events, 151.8 us)
Async XLA Ops:
  6.5 33.8 %copy-start.9 = (bf16[512,128]{1,0:T(8,128)(2,1)S(1)}, bf16[512,128]{1,0:T(8,128)(2,1)}, u32[]{:S(2)}) copy-start(bf16[512,128]{1,0:T(8,128)(2,1)} %param.4) | copy-start | bytes 393220
  6.5 149.7 %reduce-scatter.4.cloned.1.call-start = ((), (), s32[]{:S(2)}) async-start(), calls=%async_computation.5 | async-start | bytes 4325376
  39.9 0.9 copy-start.12
  49.1 107.1 %copy-start.13 = (f32[32]{0:T(128)S(1)}, f32[32]{0:T(128)}, u32[]{:S(2)}) copy-start(f32[32]{0:T(128)} %param.6) | copy-start | bytes 388
  50.5 23.6 %all-to-all-start = ((f32[32,1,1536]{2,1,0:T(1,128)}), f32[32,1,1536]{2,1,0:T(1,128)S(1)}, u32[]{:S(2)}, u32[]{:S(2)}) async-start(f32[32,1,1536]{2,1,0:T(1,128)} %broadcast_in_dim.18), calls=%async_computation | async-start | bytes 393216 | tf_op jit(solution)/shard_map/all_to_all | solution.py:19
  65.8 182.0 %all-gather.2.cloned.1.call-start = ((), (), s32[]{:S(2)}) async-start(), calls=%async_computation.4 | async-start | bytes 4325376 | tf_op jit(solution)/shard_map/all_gather | solution.py:99
  185.5 452.0 %all-to-all-start.2 = ((f32[32,512,32]{1,2,0:T(8,128)}), f32[32,512,32]{1,2,0:T(8,128)S(1)}, u32[]{:S(2)}, u32[]{:S(2)}) async-start(f32[32,512,32]{1,2,0:T(8,128)} %broadcast_in_dim.24), calls=%async_computation.2 | async-start | bytes 4194304 | tf_op jit(solution)/shard_map/all_to_all | solution.py:19
  258.3 1.9 copy-start
  266.5 1.0 copy-start.5
  412.6 3.0 copy-start.10
  416.1 9.7 %copy-start.6 = (f32[128,512]{0,1:T(8,128)}, f32[128,512]{0,1:T(8,128)S(1)}, u32[]{:S(2)}) copy-start(f32[128,512]{0,1:T(8,128)S(1)} %copy.151) | copy-start | bytes 786436
  421.5 4.3 copy-start.7
  423.1 2.7 copy-start.8
  425.8 1.6 copy-start.3
  433.4 1.0 copy-start.4
  446.1 0.6 copy-start.11
  526.7 1.2 copy-start.1
  526.7 1.5 copy-start.2
Sparse Core Ops, SparseCore 0:
  49.3 106.8 reduce-scatter.3
  183.9 63.8 all-gather.1
where the time goes:
time: 667 us; the launch traced here: 661 us
  other arithmetic  295 us (44%)
  waiting for transfers between devices  144 us (22%)
  local copies, waits for them, and re-layouts  81.4 us (12%)
  blocking collectives  55.6 us (8%)
  matrix products  41.1 us (6%)
  starting transfers between devices  24.2 us (4%)
  between operations  19.4 us (3%)
    another operation x3, other arithmetic, body(): jax.scipy.linalg.solve_triangular(diag_factor, wide_rows.T, lower=True)  82 us
    unnamed x3, waiting for transfers between devices  81.9 us
    another operation x15, other arithmetic, panel_cholesky(): bottom = jnp.linalg.cholesky(rest)  81.5 us
    another operation x14, other arithmetic, panel_cholesky(): top = jnp.linalg.cholesky(block[:panel, :panel])  79 us
    all_gather x1, waiting for transfers between devices, body(): by_cols = lax.all_gather(by_rows, 'col', axis=1, tiled=True)  53.5 us
    another operation x3, other arithmetic, panel_cholesky(): jax.scipy.linalg.solve_triangular(top, block[panel:, :panel].T, lower=True)  41.7 us
    another operation x36, local copies, waits for them, and re-layouts  40.7 us
    all_gather x1, blocking collectives, in_one_piece(): whole = lax.all_gather(both, axis, axis=dim, tiled=True)  31.8 us
  transfers between devices with their start and end apart: 4, of which 3 were waited for; matrix products, arithmetic and copies ran while one was open for 58% of the time, Pallas kernels for 0%

commit v1 on v0

--- a/solution.py
+++ b/solution.py
@@ -1,10 +1,68 @@
 import jax
 import jax.numpy as jnp
 from jax import lax
+from jax.experimental import pallas as pl
+from jax.experimental.pallas import tpu as pltpu
 from jax.sharding import PartitionSpec as P
 
 EDGES = 4096
 PANEL = 512
+BLK = 128
+SUB = 8
+HI = lax.Precision.HIGHEST
+TN = (((0,), (0,)), ((), ()))
+
+
+def _chol_rows_kernel(a_ref, o_ref):
+    n, width = a_ref.shape[0], a_ref.shape[1]
+    o_ref[...] = a_ref[...]
+    nb = n // BLK
+    for k in range(nb):
+        r0 = k * BLK
+        m = width - r0
+
+        def sub_panel(p, carry, r0=r0, m=m):
+            base = pl.multiple_of(p * SUB, SUB)
+            rows = o_ref[pl.ds(r0 + base, SUB), pl.ds(r0, m)]
+            lane = lax.broadcasted_iota(jnp.int32, (SUB, m), 1)
+            sub = lax.broadcasted_iota(jnp.int32, (SUB, m), 0)
+            lane_d = lax.broadcasted_iota(jnp.int32, (SUB, BLK), 1)
+            sub_d = lax.broadcasted_iota(jnp.int32, (SUB, BLK), 0)
+            pick = lane_d == base + sub_d
+            sub_c = lax.broadcasted_iota(jnp.int32, (SUB, 1), 0)
+            for t in range(SUB):
+                rowt = jnp.broadcast_to(rows[t:t + 1, :], (SUB, m))
+                c = jnp.sum(jnp.where(pick, rowt[:, :BLK], 0.0), axis=1, keepdims=True)
+                piv = jnp.sum(jnp.where(sub_c == t, c, 0.0), axis=0, keepdims=True)
+                inv = 1.0 / jnp.sqrt(piv)
+                u = jnp.where(lane >= base + t, rowt * inv, 0.0)
+                rows = jnp.where(sub > t, rows - (c * (inv * inv)) * rowt,
+                                 jnp.where(sub == t, u, rows))
+            o_ref[pl.ds(r0 + base, SUB), pl.ds(r0, m)] = rows
+            upd = lax.dot_general(rows[:, :BLK], rows, TN, precision=HI,
+                                  preferred_element_type=jnp.float32)
+            blk = o_ref[pl.ds(r0, BLK), pl.ds(r0, m)]
+            below = lax.broadcasted_iota(jnp.int32, (BLK, m), 0) >= base + SUB
+            o_ref[pl.ds(r0, BLK), pl.ds(r0, m)] = jnp.where(below, blk - upd, blk)
+            return carry
+
+        lax.fori_loop(0, BLK // SUB, sub_panel, 0)
+        for j in range(k + 1, nb):
+            c0 = j * BLK
+            coef = o_ref[pl.ds(r0, BLK), pl.ds(c0, BLK)]
+            right = o_ref[pl.ds(r0, BLK), pl.ds(c0, width - c0)]
+            upd = lax.dot_general(coef, right, TN, precision=HI,
+                                  preferred_element_type=jnp.float32)
+            o_ref[pl.ds(c0, BLK), pl.ds(c0, width - c0)] -= upd
+
+
+def chol_rows(aug, interpret=False):
+    return pl.pallas_call(
+        _chol_rows_kernel,
+        out_shape=jax.ShapeDtypeStruct(aug.shape, jnp.float32),
+        compiler_params=pltpu.CompilerParams(vmem_limit_bytes=48 * 1024 * 1024),
+        interpret=interpret,
+    )(aug)
 
 
 def in_one_piece(arrays, axis, dim, along):
@@ -56,18 +114,6 @@
     return parts.reshape(groups, count, width).transpose(1, 0, 2).reshape(groups * count, width)
 
 
-def panel_cholesky(block, panel):
-    top = jnp.linalg.cholesky(block[:panel, :panel])
-    lower_left = jax.scipy.linalg.solve_triangular(top, block[panel:, :panel].T, lower=True).T
-    rest = block[panel:, panel:] - jnp.dot(
-        lower_left, lower_left.T, precision=lax.Precision.HIGHEST
-    )
-    bottom = jnp.linalg.cholesky(rest)
-    upper = jnp.concatenate([top, jnp.zeros((panel, block.shape[0] - panel), jnp.float32)], axis=1)
-    lower = jnp.concatenate([lower_left, bottom], axis=1)
-    return jnp.concatenate([upper, lower], axis=0)
-
-
 def body(feats, prior_factor, ridge):
     groups = lax.axis_size("row")
     lanes = lax.axis_size("col")
@@ -98,11 +144,16 @@
     by_rows = gather_directly(head, "row", 0)
     by_cols = lax.all_gather(by_rows, "col", axis=1, tiled=True)
     square = subject_rows(by_cols, groups, leading)
-    diag_factor = panel_cholesky(square, PANEL)
     wide_rows = gather_directly(system, "col", 1)
-    solved = jax.scipy.linalg.solve_triangular(diag_factor, wide_rows.T, lower=True).T
-    factor = lax.dynamic_slice_in_dim(solved, col_start, cols_here, 1)
-    return factor
+    n = square.shape[0]
+    i = lax.broadcasted_iota(jnp.int32, (n, n), 0)
+    j = lax.broadcasted_iota(jnp.int32, (n, n), 1)
+    flipped = square.T
+    same = (i < PANEL) == (j < PANEL)
+    sym = jnp.where(same, (square + flipped) * 0.5, jnp.where(i < j, flipped, square))
+    done = chol_rows(jnp.concatenate([sym, wide_rows.T], axis=1))
+    solved_t = lax.dynamic_slice_in_dim(done[:, n:], col_start, cols_here, 0)
+    return solved_t.T
 
 
 def solution(mesh):

time: 667 us -> 492 us (0.74)
  other arithmetic: 295 us -> 16.5 us
  Pallas kernels: 0 us -> 204 us
  local copies, waits for them, and re-layouts: 81.4 us -> 31.7 us
  matrix products: 41.1 us -> 1.82 us
    another operation x35 -> x0, other arithmetic: 284 us -> none  [the longest x3 82 us: body(): jax.scipy.linalg.solve_triangular(diag_factor, wide_rows.T, lower=True)]
    pallas_call x0 -> x1, Pallas kernels: none -> 204 us  [chol_rows(): pl.pallas_call(_chol_rows_kernel, out_shape=jax.ShapeDtypeStruct(aug.shap...]
    another operation x51 -> x0, local copies, waits for them, and re-layouts: 43 us -> none
    another operation x34 -> x0, matrix products: 37 us -> none  [the longest x15 15.5 us: body(): jax.scipy.linalg.solve_triangular(diag_factor, wide_rows.T, lower=True)]
    unnamed x36 -> x11, local copies, waits for them, and re-layouts: 18.9 us -> 6.26 us
  transfers between devices with their start and end apart: 4 -> 4, of which waited for: 3 -> 3; matrix products, arithmetic and copies ran while one was open for 58% -> 5% of each run, Pallas kernels for 0% -> 0%
where the time goes in v1:
time: 492 us; the launch traced here: 491 us
  Pallas kernels  204 us (41%)
  waiting for transfers between devices  143 us (29%)
  blocking collectives  55.6 us (11%)
  local copies, waits for them, and re-layouts  31.7 us (6%)
  starting transfers between devices  24.2 us (5%)
  other arithmetic  16.5 us (3%)
  between operations  13.6 us (3%)
    pallas_call x1, Pallas kernels, chol_rows(): pl.pallas_call(_chol_rows_kernel, out_shape=jax.ShapeDtypeStruct(aug.shap...  204 us
    unnamed x3, waiting for transfers between devices  81.4 us
    all_gather x1, waiting for transfers between devices, body(): by_cols = lax.all_gather(by_rows, 'col', axis=1, tiled=True)  53.4 us
    all_gather x1, blocking collectives, in_one_piece(): whole = lax.all_gather(both, axis, axis=dim, tiled=True)  31.8 us
    all_to_all x2, starting transfers between devices, copy_for_each(): lax.all_to_all(jnp.broadcast_to(x[None], (count, *x.shape)), axis, 0, 0,...  24.2 us
    all_to_all x1, blocking collectives, copy_for_each(): lax.all_to_all(jnp.broadcast_to(x[None], (count, *x.shape)), axis, 0, 0,...  23.8 us
  transfers between devices with their start and end apart: 4, of which 3 were waited for; matrix products, arithmetic and copies ran while one was open for 5% of the time, Pallas kernels for 0%

profile of v1, /device:TPU:1, one launch (start us, length us, event | category | flops | bytes accessed | tf_op | source)
XLA Modules:
  0.0 490.8 jit_solution(18383925937693508259)
XLA Ops:
  6.5 0.8 slice.25
  7.4 0.7 slice.24
  8.2 31.8 %all_gather.6 = bf16[1024,192]{1,0:T(8,128)(2,1)S(1)} all-gather(bf16[64,192]{1,0:T(8,128)(2,1)S(1)} %pad_maximum_fusion.2), channel_id=1, replica_groups=mesh['row'=16,'col'=32] {'row'}, dimensions={0}, use_global_device_ids=true | all-gather | bytes 417792 | tf_op jit(solution)/shard_map/all_gather | solution.py:71
  40.4 1.3 convolution_bitcast_fusion.1
  42.2 2.5 pad_maximum_fusion.1
  44.7 5.4 %copy.69 = f32[1024,1024]{0,1:T(8,128)} copy(f32[1024,1024]{1,0:T(8,128)} %pad_maximum_fusion.1) | data formatting | bytes 8388608
  51.1 0.8 broadcast_in_dim.16
  51.9 15.3 %all-to-all-start = ((f32[32,1,1536]{2,1,0:T(1,128)}), f32[32,1,1536]{2,1,0:T(1,128)S(1)}, u32[]{:S(2)}, u32[]{:S(2)}) async-start(f32[32,1,1536]{2,1,0:T(1,128)} %broadcast_in_dim.16), calls=%async_computation | async-start | bytes 393216 | tf_op jit(solution)/shard_map/all_to_all | solution.py:77
  67.3 8.2 %all-to-all-done = f32[32,1,1536]{2,1,0:T(1,128)S(1)} async-done(((f32[32,1,1536]{2,1,0:T(1,128)}), f32[32,1,1536]{2,1,0:T(1,128)S(1)}, u32[]{:S(2)}, u32[]{:S(2)}) %all-to-all-start) | async-done | bytes 196640 | tf_op jit(solution)/shard_map/all_to_all | solution.py:77
  75.7 81.4 %reduce-scatter.4.cloned.1.call-done = f32[32,1024]{1,0:T(8,128)} async-done(((f32[1024,1024]{1,0:T(8,128)}), f32[32,1024]{1,0:T(8,128)}) %reduce-scatter.4.cloned.1.call-update) | async-done | bytes 131088
  157.1 1.0 slice_subtract_fusion
  158.3 23.8 %all_to_all.16 = f32[16,1,2048]{2,1,0:T(1,128)S(1)} all-to-all(f32[16,1,2048]{2,1,0:T(1,128)S(1)} %reshape.46), channel_id=1, replica_groups=mesh['row'=16,'col'=32] {'row'}, dimensions={0} | all-to-all | bytes 262144 | tf_op jit(solution)/shard_map/all_to_all | solution.py:77
  182.7 0.9 reduce.2
  183.9 0.8 reshape.40
  184.7 1.6 broadcast_in_dim.20
  186.3 8.8 %all-to-all-start.2 = ((f32[32,512,32]{1,2,0:T(8,128)}), f32[32,512,32]{1,2,0:T(8,128)S(1)}, u32[]{:S(2)}, u32[]{:S(2)}) async-start(f32[32,512,32]{1,2,0:T(8,128)} %broadcast_in_dim.20), calls=%async_computation.2 | async-start | bytes 4194304 | tf_op jit(solution)/shard_map/all_to_all | solution.py:77
  195.1 53.4 %all-gather.2.cloned.1.call-done = f32[1024,1024]{0,1:T(8,128)} async-done(((f32[1024,32]{0,1:T(8,128)}), f32[1024,1024]{0,1:T(8,128)}) %all-gather.2.cloned.1.call-update) | async-done | bytes 4194320 | tf_op jit(solution)/shard_map/all_gather | solution.py:145
  248.6 5.4 %copy.66 = f32[1024,1024]{1,0:T(8,128)} copy(f32[1024,1024]{0,1:T(8,128)} %all-gather.2.cloned.1.call-done) | data formatting | bytes 8388608 | tf_op jit(solution)/shard_map/all_gather | solution.py:145
  253.9 6.6 %copy.67 = f32[64,16,1024]{2,1,0:T(8,128)} copy(f32[64,16,1024]{2,0,1:T(8,128)} %bitcast.46) | data formatting | bytes 8388608 | tf_op jit(solution)/shard_map/transpose | solution.py:114
  260.5 5.3 %copy.68 = f32[1024,1024]{0,1:T(8,128)} copy(f32[1024,1024]{1,0:T(8,128)} %bitcast.44) | data formatting | bytes 8388608 | tf_op jit(solution)/shard_map/reshape | solution.py:114
  265.8 6.2 %fusion.1 = f32[1024,1024]{1,0:T(8,128)} fusion(f32[1024,1024]{0,1:T(8,128)} %copy.68, pred[1024]{0:T(1024)(128)(4,1)S(1)} %iota_compare_fusion.1, f32[64,16,1024]{2,1,0:T(8,128)} %copy.67), kind=kLoop, calls=%fused_computation.5 | loop fusion | flops 6291456 | bytes 12583936 | tf_op jit(solution)/shard_map/jit(_where)/select_n | solution.py:153
  272.0 5.4 %pad_maximum_fusion.a_ref = f32[1024,1536]{1,0:T(8,128)} fusion(f32[1024,512]{1,0:T(8,128)S(1)} %bitcast.47, f32[1024,1024]{1,0:T(8,128)} %fusion.1), kind=kLoop, calls=%fused_computation | loop fusion | flops 1572864 | bytes 12582912 | tf_op jit(solution)/shard_map/concatenate | solution.py:154
  277.5 204.3 %shard_map.37 = f32[1024,1536]{1,0:T(8,128)} custom-call(f32[1024,1536]{1,0:T(8,128)} %pad_maximum_fusion.a_ref), custom_call_target="tpu_custom_call" | custom-call | tf_op jit(solution)/shard_map/pallas_call | solution.py:60
  481.7 1.6 slice-done
  (38 shorter events, 3.9 us)
Async XLA Ops:
  6.5 35.2 %copy-start.1 = (bf16[512,64]{0,1:T(8,128)(2,1)S(1)}, bf16[512,64]{0,1:T(8,128)(2,1)}, u32[]{:S(2)}) copy-start(bf16[512,64]{0,1:T(8,128)(2,1)} %param.4) | copy-start | bytes 196612
  6.5 150.6 %reduce-scatter.4.cloned.1.call-start = ((), (), s32[]{:S(2)}) async-start(), calls=%async_computation.5 | async-start | bytes 4325376
  50.1 0.9 copy-start
  50.1 107.1 %copy-start.2 = (f32[32]{0:T(128)S(1)}, f32[32]{0:T(128)}, u32[]{:S(2)}) copy-start(f32[32]{0:T(128)} %param.5) | copy-start | bytes 388
  51.9 23.6 %all-to-all-start = ((f32[32,1,1536]{2,1,0:T(1,128)}), f32[32,1,1536]{2,1,0:T(1,128)S(1)}, u32[]{:S(2)}, u32[]{:S(2)}) async-start(f32[32,1,1536]{2,1,0:T(1,128)} %broadcast_in_dim.16), calls=%async_computation | async-start | bytes 393216 | tf_op jit(solution)/shard_map/all_to_all | solution.py:77
  67.2 181.4 %all-gather.2.cloned.1.call-start = ((), (), s32[]{:S(2)}) async-start(), calls=%async_computation.4 | async-start | bytes 4325376 | tf_op jit(solution)/shard_map/all_gather | solution.py:145
  186.3 85.7 %all-to-all-start.2 = ((f32[32,512,32]{1,2,0:T(8,128)}), f32[32,512,32]{1,2,0:T(8,128)S(1)}, u32[]{:S(2)}, u32[]{:S(2)}) async-start(f32[32,512,32]{1,2,0:T(8,128)} %broadcast_in_dim.20), calls=%async_computation.2 | async-start | bytes 4194304 | tf_op jit(solution)/shard_map/all_to_all | solution.py:77
  481.7 1.6 slice-start
Sparse Core Ops, SparseCore 0:
  50.2 106.8 reduce-scatter.3
  184.8 63.7 all-gather.1

commit v2 on v1

--- a/solution.py
+++ b/solution.py
@@ -13,40 +13,61 @@
 TN = (((0,), (0,)), ((), ()))
 
 
-def _chol_rows_kernel(a_ref, o_ref):
+def _diag(d_ref):
+    wide = 2 * BLK
+    lane = lax.broadcasted_iota(jnp.int32, (SUB, wide), 1)
+    sub = lax.broadcasted_iota(jnp.int32, (SUB, wide), 0)
+    lane_d = lax.broadcasted_iota(jnp.int32, (SUB, BLK), 1)
+    sub_d = lax.broadcasted_iota(jnp.int32, (SUB, BLK), 0)
+    rows = d_ref[0:SUB, :]
+    for p in range(BLK // SUB):
+        base = p * SUB
+        pick = lane_d == base + sub_d
+        for t in range(SUB):
+            rowt = jnp.broadcast_to(rows[t:t + 1, :], (SUB, wide))
+            head = rowt[:, :BLK]
+            c = jnp.sum(jnp.where(pick, head, 0.0), axis=1, keepdims=True)
+            piv = jnp.sum(jnp.where(lane_d == base + t, head, 0.0), axis=1, keepdims=True)
+            inv = lax.rsqrt(piv)
+            u = jnp.where(lane >= base + t, rowt * inv, 0.0)
+            rows = jnp.where(sub > t, rows - (c * (inv * inv)) * rowt,
+                             jnp.where(sub == t, u, rows))
+        d_ref[base:base + SUB, :] = rows
+        nb0 = base + SUB
+        if nb0 < BLK:
+            nxt = d_ref[nb0:nb0 + SUB, :]
+            pick2 = lane_d == nb0 + sub_d
+            for t in range(SUB):
+                rowt = jnp.broadcast_to(rows[t:t + 1, :], (SUB, wide))
+                coef = jnp.sum(jnp.where(pick2, rowt[:, :BLK], 0.0), axis=1, keepdims=True)
+                nxt = nxt - coef * rowt
+            lo = nb0 + SUB
+            if lo < BLK:
+                upd = lax.dot_general(rows[:, :BLK], rows, TN, precision=HI,
+                                      preferred_element_type=jnp.float32)
+                d_ref[lo:BLK, :] = d_ref[lo:BLK, :] - upd[lo:, :]
+            rows = nxt
+
+
+def _chol_rows_kernel(a_ref, o_ref, d_ref):
     n, width = a_ref.shape[0], a_ref.shape[1]
     o_ref[...] = a_ref[...]
     nb = n // BLK
+    wide = 2 * BLK
+    eye = (lax.broadcasted_iota(jnp.int32, (BLK, BLK), 0)
+           == lax.broadcasted_iota(jnp.int32, (BLK, BLK), 1)).astype(jnp.float32)
     for k in range(nb):
         r0 = k * BLK
         m = width - r0
+        d_ref[:, :BLK] = o_ref[pl.ds(r0, BLK), pl.ds(r0, BLK)]
+        d_ref[:, BLK:] = eye
 
-        def sub_panel(p, carry, r0=r0, m=m):
-            base = pl.multiple_of(p * SUB, SUB)
-            rows = o_ref[pl.ds(r0 + base, SUB), pl.ds(r0, m)]
-            lane = lax.broadcasted_iota(jnp.int32, (SUB, m), 1)
-            sub = lax.broadcasted_iota(jnp.int32, (SUB, m), 0)
-            lane_d = lax.broadcasted_iota(jnp.int32, (SUB, BLK), 1)
-            sub_d = lax.broadcasted_iota(jnp.int32, (SUB, BLK), 0)
-            pick = lane_d == base + sub_d
-            sub_c = lax.broadcasted_iota(jnp.int32, (SUB, 1), 0)
-            for t in range(SUB):
-                rowt = jnp.broadcast_to(rows[t:t + 1, :], (SUB, m))
-                c = jnp.sum(jnp.where(pick, rowt[:, :BLK], 0.0), axis=1, keepdims=True)
-                piv = jnp.sum(jnp.where(sub_c == t, c, 0.0), axis=0, keepdims=True)
-                inv = 1.0 / jnp.sqrt(piv)
-                u = jnp.where(lane >= base + t, rowt * inv, 0.0)
-                rows = jnp.where(sub > t, rows - (c * (inv * inv)) * rowt,
-                                 jnp.where(sub == t, u, rows))
-            o_ref[pl.ds(r0 + base, SUB), pl.ds(r0, m)] = rows
-            upd = lax.dot_general(rows[:, :BLK], rows, TN, precision=HI,
-                                  preferred_element_type=jnp.float32)
-            blk = o_ref[pl.ds(r0, BLK), pl.ds(r0, m)]
-            below = lax.broadcasted_iota(jnp.int32, (BLK, m), 0) >= base + SUB
-            o_ref[pl.ds(r0, BLK), pl.ds(r0, m)] = jnp.where(below, blk - upd, blk)
-            return carry
-
-        lax.fori_loop(0, BLK // SUB, sub_panel, 0)
+        _diag(d_ref)
+        o_ref[pl.ds(r0, BLK), pl.ds(r0, BLK)] = d_ref[:, :BLK]
+        if m > BLK:
+            rest = o_ref[pl.ds(r0, BLK), pl.ds(r0 + BLK, m - BLK)]
+            o_ref[pl.ds(r0, BLK), pl.ds(r0 + BLK, m - BLK)] = jnp.dot(
+                d_ref[:, BLK:], rest, precision=HI, preferred_element_type=jnp.float32)
         for j in range(k + 1, nb):
             c0 = j * BLK
             coef = o_ref[pl.ds(r0, BLK), pl.ds(c0, BLK)]
@@ -60,6 +81,7 @@
     return pl.pallas_call(
         _chol_rows_kernel,
         out_shape=jax.ShapeDtypeStruct(aug.shape, jnp.float32),
+        scratch_shapes=[pltpu.VMEM((BLK, 2 * BLK), jnp.float32)],
         compiler_params=pltpu.CompilerParams(vmem_limit_bytes=48 * 1024 * 1024),
         interpret=interpret,
     )(aug)

time: 492 us -> 408 us (0.83); the launches traced: 491 us -> 401 us
  Pallas kernels: 204 us -> 115 us
    pallas_call x1, Pallas kernels: 204 us -> 115 us  [chol_rows(): pl.pallas_call(_chol_rows_kernel, out_shape=jax.ShapeDtypeStruct(aug.shap...]
  transfers between devices with their start and end apart: 4 -> 4, of which waited for: 3 -> 3; matrix products, arithmetic and copies ran while one was open for 5% -> 7% of each run, Pallas kernels for 0% -> 0%
where the time goes in v2:
time: 408 us; the launch traced here: 401 us
  waiting for transfers between devices  143 us (35%)
  Pallas kernels  115 us (28%)
  blocking collectives  55.6 us (14%)
  local copies, waits for them, and re-layouts  31.8 us (8%)
  starting transfers between devices  24.2 us (6%)
  other arithmetic  16.5 us (4%)
  between operations  13.8 us (3%)
    pallas_call x1, Pallas kernels, chol_rows(): pl.pallas_call(_chol_rows_kernel, out_shape=jax.ShapeDtypeStruct(aug.shap...  115 us
    unnamed x3, waiting for transfers between devices  81.4 us
    all_gather x1, waiting for transfers between devices, body(): by_cols = lax.all_gather(by_rows, 'col', axis=1, tiled=True)  53.5 us
    all_gather x1, blocking collectives, in_one_piece(): whole = lax.all_gather(both, axis, axis=dim, tiled=True)  31.8 us
    all_to_all x2, starting transfers between devices, copy_for_each(): lax.all_to_all(jnp.broadcast_to(x[None], (count, *x.shape)), axis, 0, 0,...  24.2 us
    all_to_all x1, blocking collectives, copy_for_each(): lax.all_to_all(jnp.broadcast_to(x[None], (count, *x.shape)), axis, 0, 0,...  23.8 us
    all_to_all x2, waiting for transfers between devices, copy_for_each(): lax.all_to_all(jnp.broadcast_to(x[None], (count, *x.shape)), axis, 0, 0,...  8.22 us
  transfers between devices with their start and end apart: 4, of which 3 were waited for; matrix products, arithmetic and copies ran while one was open for 7% of the time, Pallas kernels for 0%

profile of v2, /device:TPU:1, one launch (start us, length us, event | category | flops | bytes accessed | tf_op | source)
XLA Modules:
  0.0 401.4 jit_solution(15003063797697205638)
XLA Ops:
  6.5 0.8 slice.25
  7.4 0.7 slice.24
  8.2 31.8 %all_gather.6 = bf16[1024,192]{1,0:T(8,128)(2,1)S(1)} all-gather(bf16[64,192]{1,0:T(8,128)(2,1)S(1)} %pad_maximum_fusion.2), channel_id=1, replica_groups=mesh['row'=16,'col'=32] {'row'}, dimensions={0}, use_global_device_ids=true | all-gather | bytes 417792 | tf_op jit(solution)/shard_map/all_gather | solution.py:93
  40.4 1.3 convolution_bitcast_fusion.1
  42.2 2.5 pad_maximum_fusion.1
  44.7 5.4 %copy.69 = f32[1024,1024]{0,1:T(8,128)} copy(f32[1024,1024]{1,0:T(8,128)} %pad_maximum_fusion.1) | data formatting | bytes 8388608
  51.1 0.8 broadcast_in_dim.16
  51.9 15.3 %all-to-all-start = ((f32[32,1,1536]{2,1,0:T(1,128)}), f32[32,1,1536]{2,1,0:T(1,128)S(1)}, u32[]{:S(2)}, u32[]{:S(2)}) async-start(f32[32,1,1536]{2,1,0:T(1,128)} %broadcast_in_dim.16), calls=%async_computation | async-start | bytes 393216 | tf_op jit(solution)/shard_map/all_to_all | solution.py:99
  67.3 8.2 %all-to-all-done = f32[32,1,1536]{2,1,0:T(1,128)S(1)} async-done(((f32[32,1,1536]{2,1,0:T(1,128)}), f32[32,1,1536]{2,1,0:T(1,128)S(1)}, u32[]{:S(2)}, u32[]{:S(2)}) %all-to-all-start) | async-done | bytes 196640 | tf_op jit(solution)/shard_map/all_to_all | solution.py:99
  75.7 81.4 %reduce-scatter.4.cloned.1.call-done = f32[32,1024]{1,0:T(8,128)} async-done(((f32[1024,1024]{1,0:T(8,128)}), f32[32,1024]{1,0:T(8,128)}) %reduce-scatter.4.cloned.1.call-update) | async-done | bytes 131088
  157.2 1.0 slice_subtract_fusion
  158.3 23.8 %all_to_all.16 = f32[16,1,2048]{2,1,0:T(1,128)S(1)} all-to-all(f32[16,1,2048]{2,1,0:T(1,128)S(1)} %reshape.46), channel_id=1, replica_groups=mesh['row'=16,'col'=32] {'row'}, dimensions={0} | all-to-all | bytes 262144 | tf_op jit(solution)/shard_map/all_to_all | solution.py:99
  182.6 0.9 reduce.2
  183.9 0.8 reshape.40
  184.7 1.6 broadcast_in_dim.20
  186.2 8.9 %all-to-all-start.2 = ((f32[32,512,32]{1,2,0:T(8,128)}), f32[32,512,32]{1,2,0:T(8,128)S(1)}, u32[]{:S(2)}, u32[]{:S(2)}) async-start(f32[32,512,32]{1,2,0:T(8,128)} %broadcast_in_dim.20), calls=%async_computation.2 | async-start | bytes 4194304 | tf_op jit(solution)/shard_map/all_to_all | solution.py:99
  195.1 53.5 %all-gather.2.cloned.1.call-done = f32[1024,1024]{0,1:T(8,128)} async-done(((f32[1024,32]{0,1:T(8,128)}), f32[1024,1024]{0,1:T(8,128)}) %all-gather.2.cloned.1.call-update) | async-done | bytes 4194320 | tf_op jit(solution)/shard_map/all_gather | solution.py:167
  248.6 5.4 %copy.66 = f32[1024,1024]{1,0:T(8,128)} copy(f32[1024,1024]{0,1:T(8,128)} %all-gather.2.cloned.1.call-done) | data formatting | bytes 8388608 | tf_op jit(solution)/shard_map/all_gather | solution.py:167
  254.0 6.6 %copy.67 = f32[64,16,1024]{2,1,0:T(8,128)} copy(f32[64,16,1024]{2,0,1:T(8,128)} %bitcast.46) | data formatting | bytes 8388608 | tf_op jit(solution)/shard_map/transpose | solution.py:136
  260.5 5.5 %copy.68 = f32[1024,1024]{0,1:T(8,128)} copy(f32[1024,1024]{1,0:T(8,128)} %bitcast.44) | data formatting | bytes 8388608 | tf_op jit(solution)/shard_map/reshape | solution.py:136
  266.0 6.2 %fusion.1 = f32[1024,1024]{1,0:T(8,128)} fusion(f32[1024,1024]{0,1:T(8,128)} %copy.68, pred[1024]{0:T(1024)(128)(4,1)S(1)} %iota_compare_fusion.1, f32[64,16,1024]{2,1,0:T(8,128)} %copy.67), kind=kLoop, calls=%fused_computation.5 | loop fusion | flops 6291456 | bytes 12583936 | tf_op jit(solution)/shard_map/jit(_where)/select_n | solution.py:175
  272.2 5.4 %pad_maximum_fusion.a_ref = f32[1024,1536]{1,0:T(8,128)} fusion(f32[1024,512]{1,0:T(8,128)S(1)} %bitcast.47, f32[1024,1024]{1,0:T(8,128)} %fusion.1), kind=kLoop, calls=%fused_computation | loop fusion | flops 1572864 | bytes 12582912 | tf_op jit(solution)/shard_map/concatenate | solution.py:176
  277.6 114.5 %shard_map.37 = f32[1024,1536]{1,0:T(8,128)} custom-call(f32[1024,1536]{1,0:T(8,128)} %pad_maximum_fusion.a_ref), custom_call_target="tpu_custom_call" | custom-call | tf_op jit(solution)/shard_map/pallas_call | solution.py:81
  392.2 1.6 slice-done
  (38 shorter events, 3.9 us)
Async XLA Ops:
  6.5 35.2 %copy-start.1 = (bf16[512,64]{0,1:T(8,128)(2,1)S(1)}, bf16[512,64]{0,1:T(8,128)(2,1)}, u32[]{:S(2)}) copy-start(bf16[512,64]{0,1:T(8,128)(2,1)} %param.4) | copy-start | bytes 196612
  6.5 150.6 %reduce-scatter.4.cloned.1.call-start = ((), (), s32[]{:S(2)}) async-start(), calls=%async_computation.5 | async-start | bytes 4325376
  50.1 0.9 copy-start
  50.1 107.1 %copy-start.2 = (f32[32]{0:T(128)S(1)}, f32[32]{0:T(128)}, u32[]{:S(2)}) copy-start(f32[32]{0:T(128)} %param.5) | copy-start | bytes 388
  51.9 23.6 %all-to-all-start = ((f32[32,1,1536]{2,1,0:T(1,128)}), f32[32,1,1536]{2,1,0:T(1,128)S(1)}, u32[]{:S(2)}, u32[]{:S(2)}) async-start(f32[32,1,1536]{2,1,0:T(1,128)} %broadcast_in_dim.16), calls=%async_computation | async-start | bytes 393216 | tf_op jit(solution)/shard_map/all_to_all | solution.py:99
  67.2 181.4 %all-gather.2.cloned.1.call-start = ((), (), s32[]{:S(2)}) async-start(), calls=%async_computation.4 | async-start | bytes 4325376 | tf_op jit(solution)/shard_map/all_gather | solution.py:167
  186.2 86.0 %all-to-all-start.2 = ((f32[32,512,32]{1,2,0:T(8,128)}), f32[32,512,32]{1,2,0:T(8,128)S(1)}, u32[]{:S(2)}, u32[]{:S(2)}) async-start(f32[32,512,32]{1,2,0:T(8,128)} %broadcast_in_dim.20), calls=%async_computation.2 | async-start | bytes 4194304 | tf_op jit(solution)/shard_map/all_to_all | solution.py:99
  392.2 1.6 slice-start
Sparse Core Ops, SparseCore 0:
  50.2 106.8 reduce-scatter.3
  184.8 63.7 all-gather.1

commit v3 on v2

--- a/solution.py
+++ b/solution.py
@@ -152,30 +152,46 @@
     update_part = jnp.dot(prior_factor, col_prior.T, preferred_element_type=jnp.float32)
     wide_feats = feats.astype(jnp.float32)
     wide_cols = col_feats.astype(jnp.float32)
-    row_sq, col_sq = together(
-        (jnp.sum(wide_feats * wide_feats, axis=1), jnp.sum(wide_cols * wide_cols, axis=1)), "col"
+    col_start = col_pos * cols_here
+    ridge_pad = lax.dynamic_update_slice_in_dim(
+        jnp.zeros((total_cols,), jnp.float32), ridge, col_start, 0)
+    row_sq, col_sq, ridge_all = together(
+        (jnp.sum(wide_feats * wide_feats, axis=1), jnp.sum(wide_cols * wide_cols, axis=1),
+         ridge_pad), "col"
     )
-    gram, update = in_one_piece_2((gram_part, update_part), "col", 1, 0)
-    col_start = col_pos * cols_here
-    own_sq = lax.dynamic_slice_in_dim(col_sq, col_start, cols_here)
-    kernel = jnp.exp(-(row_sq[:, None] + own_sq[None, :] - 2.0 * gram) / EDGES)
-    subject = lax.broadcasted_iota(jnp.int32, (rows_here, cols_here), 0) * groups + row_pos
-    column = lax.broadcasted_iota(jnp.int32, (rows_here, cols_here), 1) + col_start
-    system = kernel + jnp.where(subject == column, ridge[None, :], jnp.zeros_like(kernel)) - update
-    head = system[:leading]
-    by_rows = gather_directly(head, "row", 0)
-    by_cols = lax.all_gather(by_rows, "col", axis=1, tiled=True)
-    square = subject_rows(by_cols, groups, leading)
-    wide_rows = gather_directly(system, "col", 1)
+
+    def system_of(gram, update, sq, first):
+        count, width = gram.shape
+        start = col_start if width == cols_here else 0
+        col_part = lax.dynamic_slice_in_dim(col_sq, start, width)
+        kernel = jnp.exp(-(sq[:, None] + col_part[None, :] - 2.0 * gram) / EDGES)
+        subject = (lax.broadcasted_iota(jnp.int32, (count, width), 0) + first) * groups + row_pos
+        column = lax.broadcasted_iota(jnp.int32, (count, width), 1) + start
+        ridge_part = ridge if width == cols_here else ridge_all
+        diag = jnp.where(subject == column, ridge_part[None, :], jnp.zeros_like(kernel))
+        return kernel + diag - update
+
+    head_gram, head_update = in_one_piece_2(
+        (gram_part[:leading], update_part[:leading]), "col", 1, 0)
+    head = system_of(head_gram, head_update, row_sq[:leading], 0)
+    by_rows = subject_rows(gather_directly(head, "row", 0), groups, leading)
+    square = lax.all_gather(by_rows, "col", axis=1, tiled=True)
+    gram_part, update_part, square = lax.optimization_barrier((gram_part, update_part, square))
     n = square.shape[0]
     i = lax.broadcasted_iota(jnp.int32, (n, n), 0)
     j = lax.broadcasted_iota(jnp.int32, (n, n), 1)
     flipped = square.T
     same = (i < PANEL) == (j < PANEL)
     sym = jnp.where(same, (square + flipped) * 0.5, jnp.where(i < j, flipped, square))
-    done = chol_rows(jnp.concatenate([sym, wide_rows.T], axis=1))
-    solved_t = lax.dynamic_slice_in_dim(done[:, n:], col_start, cols_here, 0)
-    return solved_t.T
+    eye = (i == j).astype(jnp.float32)
+    done = chol_rows(jnp.concatenate([sym, eye], axis=1))
+    inv_t = lax.dynamic_slice_in_dim(done[:, n:], col_start, cols_here, 0)
+
+    both = lax.psum(jnp.concatenate([gram_part, update_part], axis=0), "col")
+    gram, update = both[:rows_here], both[rows_here:]
+    system = system_of(gram, update, row_sq, 0)
+    return lax.dot_general(system, inv_t, (((1,), (1,)), ((), ())), precision=HI,
+                           preferred_element_type=jnp.float32)
 
 
 def solution(mesh):

time: 408 us -> 397 us (0.973)
  local copies, waits for them, and re-layouts: 31.8 us -> 18.1 us
  starting transfers between devices: 24.2 us -> 15.4 us
  Pallas kernels: 115 us -> 122 us
  matrix products: 1.82 us -> 7.54 us
    all_to_all x2 -> x1, starting transfers between devices: 24.2 us -> 15.3 us  [copy_for_each(): lax.all_to_all(jnp.broadcast_to(x[None], (count, *x.shape)), axis, 0, 0,...]
    pallas_call x1, Pallas kernels: 115 us -> 122 us  [chol_rows(): pl.pallas_call(_chol_rows_kernel, out_shape=jax.ShapeDtypeStruct(aug.shap...]
    unnamed x3 -> x4, waiting for transfers between devices: 81.4 us -> 75.1 us
    transpose x2 -> x3, local copies, waits for them, and re-layouts: 6.73 us -> 0.48 us  [subject_rows(): parts.reshape(groups, count, width).transpose(1, 0, 2)]
    dot_general x0 -> x1, matrix products: none -> 5.67 us  [body(): lax.dot_general(system, inv_t, (((1,), (1,)), ((), ())), precision=HI, pr...]
    all_gather x1 -> x0, local copies, waits for them, and re-layouts: 5.36 us -> none  [body(): by_cols = lax.all_gather(by_rows, 'col', axis=1, tiled=True)]
    optimization_barrier x0 -> x1, local copies, waits for them, and re-layouts: none -> 5.34 us  [body(): lax.optimization_barrier((gram_part, update_part, square))]
    reshape x2, local copies, waits for them, and re-layouts: 5.66 us -> 1.01 us  [subject_rows(): parts.reshape(groups, count, width).transpose(1, 0, 2)]
  transfers between devices with their start and end apart: 4 -> 4, of which waited for: 3 -> 4; matrix products, arithmetic and copies ran while one was open for 7% -> 6% of each run, Pallas kernels for 0% -> 31%
where the time goes in v3:
time: 397 us; the launch traced here: 392 us
  waiting for transfers between devices  142 us (36%)
  Pallas kernels  122 us (31%)
  blocking collectives  55.6 us (14%)
  local copies, waits for them, and re-layouts  18.1 us (5%)
  other arithmetic  17.3 us (4%)
  starting transfers between devices  15.4 us (4%)
  between operations  13.6 us (3%)
  matrix products  7.54 us (2%)
    pallas_call x1, Pallas kernels, chol_rows(): pl.pallas_call(_chol_rows_kernel, out_shape=jax.ShapeDtypeStruct(aug.shap...  122 us
    unnamed x4, waiting for transfers between devices  75.1 us
    all_gather x1, waiting for transfers between devices, body(): square = lax.all_gather(by_rows, 'col', axis=1, tiled=True)  56.2 us
    all_gather x1, blocking collectives, in_one_piece(): whole = lax.all_gather(both, axis, axis=dim, tiled=True)  31.8 us
    all_to_all x1, blocking collectives, copy_for_each(): lax.all_to_all(jnp.broadcast_to(x[None], (count, *x.shape)), axis, 0, 0,...  23.9 us
    all_to_all x1, starting transfers between devices, copy_for_each(): lax.all_to_all(jnp.broadcast_to(x[None], (count, *x.shape)), axis, 0, 0,...  15.3 us
    all_to_all x1, waiting for transfers between devices, copy_for_each(): lax.all_to_all(jnp.broadcast_to(x[None], (count, *x.shape)), axis, 0, 0,...  9.54 us
  transfers between devices with their start and end apart: 4, of which 4 were waited for; matrix products, arithmetic and copies ran while one was open for 6% of the time, Pallas kernels for 31%

profile of v3, /device:TPU:1, one launch (start us, length us, event | category | flops | bytes accessed | tf_op | source)
XLA Modules:
  0.0 391.8 jit_solution(17088983449204757059)
XLA Ops:
  6.5 0.8 slice.41
  7.4 0.7 slice.40
  8.2 31.8 %all_gather.6 = bf16[1024,192]{1,0:T(8,128)(2,1)S(1)} all-gather(bf16[64,192]{1,0:T(8,128)(2,1)S(1)} %pad_maximum_fusion.3), channel_id=1, replica_groups=mesh['row'=16,'col'=32] {'row'}, dimensions={0}, use_global_device_ids=true | all-gather | bytes 417792 | tf_op jit(solution)/shard_map/all_gather | solution.py:93
  40.4 1.4 convolution_bitcast_fusion.1
  42.3 1.3 copy-done.1
  43.7 1.0 copy.59
  45.5 0.9 broadcast_in_dim.24
  46.4 15.3 %all-to-all-start = ((f32[32,1,2560]{2,1,0:T(1,128)}), f32[32,1,2560]{2,1,0:T(1,128)S(1)}, u32[]{:S(2)}, u32[]{:S(2)}) async-start(f32[32,1,2560]{2,1,0:T(1,128)} %broadcast_in_dim.24), calls=%async_computation | async-start | bytes 655360 | tf_op jit(solution)/shard_map/all_to_all | solution.py:99
  61.8 9.5 %all-to-all-done = f32[32,1,2560]{2,1,0:T(1,128)S(1)} async-done(((f32[32,1,2560]{2,1,0:T(1,128)}), f32[32,1,2560]{2,1,0:T(1,128)S(1)}, u32[]{:S(2)}, u32[]{:S(2)}) %all-to-all-start) | async-done | bytes 327712 | tf_op jit(solution)/shard_map/all_to_all | solution.py:99
  71.7 75.1 %reduce-scatter.4.cloned.1.call-done = f32[32,128]{1,0:T(8,128)} async-done(((f32[1024,128]{1,0:T(8,128)}), f32[32,128]{1,0:T(8,128)}) %reduce-scatter.4.cloned.1.call-update) | async-done | bytes 16400
  146.8 0.9 slice_subtract_fusion.2
  147.8 23.9 %all_to_all.11 = f32[16,1,2048]{2,1,0:T(1,128)S(1)} all-to-all(f32[16,1,2048]{2,1,0:T(1,128)S(1)} %reshape.36), channel_id=1, replica_groups=mesh['row'=16,'col'=32] {'row'}, dimensions={0} | all-to-all | bytes 262144 | tf_op jit(solution)/shard_map/all_to_all | solution.py:99
  172.3 0.9 reduce.2
  173.6 0.8 copy.56
  174.5 56.2 %all-gather.2.cloned.1.call-done = f32[1024,1024]{0,1:T(8,128)} async-done(((f32[1024,32]{0,1:T(8,128)}), f32[1024,1024]{0,1:T(8,128)}) %all-gather.2.cloned.1.call-update) | async-done | bytes 4194320 | tf_op jit(solution)/shard_map/all_gather | solution.py:178
  230.8 4.1 %pad_maximum_fusion.1 = f32[1024,1024]{1,0:T(8,128)} fusion(f32[512,1024]{1,0:T(8,128)} %copy-done.1, f32[512,1024]{1,0:T(8,128)S(1)} %convolution_bitcast_fusion.1), kind=kLoop, calls=%fused_computation.1 | loop fusion | flops 1048576 | bytes 8388608 | tf_op jit(solution)/shard_map/concatenate | solution.py:190
  234.9 2.5 fusion.2
  237.4 5.3 %copy.57 = f32[1024,1024]{1,0:T(8,128)} copy(f32[1024,1024]{0,1:T(8,128)} %all-gather.2.cloned.1.call-done) | data formatting | bytes 8388608 | tf_op jit(solution)/shard_map/optimization_barrier | solution.py:179
  242.8 4.5 %fusion.1 = f32[1024,1024]{1,0:T(8,128)S(1)} fusion(f32[1024,1024]{1,0:T(8,128)} %copy.57, f32[1024,1024]{0,1:T(8,128)} %all-gather.2.cloned.1.call-done, pred[1024]{0:T(1024)(128)(4,1)S(1)} %iota_compare_fusion.4), kind=kLoop, calls=%fused_computation.5 | loop fusion | flops 6291456 | bytes 12583936 | tf_op jit(solution)/shard_map/jit(_where)/select_n | solution.py:185
  247.4 3.8 pad_maximum_fusion.a_ref
  251.2 121.8 %shard_map.37 = f32[1024,2048]{1,0:T(8,128)} custom-call(f32[1024,2048]{1,0:T(8,128)} %pad_maximum_fusion.a_ref), custom_call_target="tpu_custom_call" | custom-call | tf_op jit(solution)/shard_map/pallas_call | solution.py:81
  373.1 4.8 %slice.63 = f32[1024,1024]{1,0:T(8,128)} slice(f32[1024,2048]{1,0:T(8,128)} %shard_map.37), slice={[0:1024], [1024:2048]} | slice | bytes 8388608 | tf_op jit(solution)/shard_map/slice | solution.py:188
  377.9 1.4 all-reduce.2.cloned.1.call-done
  379.3 5.7 %fusion.3 = f32[512,32]{0,1:T(8,128)} fusion(f32[1024,1024]{1,0:T(8,128)} %all-reduce.2.cloned.1.call-done, f32[1024]{0:T(1024)S(1)} %get-tuple-element.11, s32[512]{0:T(512)S(1)} %multiply_add_fusion, f32[1024]{0:T(1024)S(1)} %get-tuple-element.12, f32[512]{0:T(512)S(1)} %slice-done, f32[1024,1024]{1,0:T(8,128)} %slice.63, s32[]{:T(128)S(6)} %select_n.20), kind=kOutput, calls=%fused_computation.10 | convolution fusion | flops 206045184 | bytes 4403204 | tf_op jit(solution)/shard_map/dot_general | solution.py:193
  (50 shorter events, 3.6 us)
Async XLA Ops:
  6.5 35.3 %copy-start.3 = (bf16[512,64]{0,1:T(8,128)(2,1)S(1)}, bf16[512,64]{0,1:T(8,128)(2,1)}, u32[]{:S(2)}) copy-start(bf16[512,64]{0,1:T(8,128)(2,1)} %param.4) | copy-start | bytes 196612
  6.5 140.2 %reduce-scatter.4.cloned.1.call-start = ((), (), s32[]{:S(2)}) async-start(), calls=%async_computation.5 | async-start | bytes 540672
  40.4 4.7 %copy-start.5 = (f32[32]{0:T(128)S(1)}, f32[32]{0:T(128)}, u32[]{:S(2)}) copy-start(f32[32]{0:T(128)} %param.5) | copy-start | bytes 388
  40.4 5.0 %copy-start.2 = (bf16[512,128]{1,0:T(8,128)(2,1)S(1)}, bf16[512,128]{1,0:T(8,128)(2,1)}, u32[]{:S(2)}) copy-start(bf16[512,128]{1,0:T(8,128)(2,1)} %param.3) | copy-start | bytes 393220
  42.3 1.3 copy-start.1
  46.4 25.0 %all-to-all-start = ((f32[32,1,2560]{2,1,0:T(1,128)}), f32[32,1,2560]{2,1,0:T(1,128)S(1)}, u32[]{:S(2)}, u32[]{:S(2)}) async-start(f32[32,1,2560]{2,1,0:T(1,128)} %broadcast_in_dim.24), calls=%async_computation | async-start | bytes 655360 | tf_op jit(solution)/shard_map/all_to_all | solution.py:99
  61.8 169.0 %all-gather.2.cloned.1.call-start = ((), (), s32[]{:S(2)}) async-start(), calls=%async_computation.3 | async-start | bytes 4325376 | tf_op jit(solution)/shard_map/all_gather | solution.py:178
  71.6 165.9 %copy-start.4 = (f32[2560]{0:T(1024)}, f32[2560]{0:T(1024)S(1)}, u32[]{:S(2)}) copy-start(f32[2560]{0:T(1024)S(1)} %reduce_sum.32) | copy-start | bytes 30724
  174.5 204.8 %all-reduce.2.cloned.1.call-start = ((), (), s32[]{:S(2)}) async-start(), calls=%async_computation.4 | async-start | bytes 8388608 | tf_op jit(solution)/shard_map/psum | solution.py:190
  242.8 4.7 %copy-start = (f32[1024,1024]{1,0:T(8,128)S(1)}, f32[1024,1024]{1,0:T(8,128)}, u32[]{:S(2)}) copy-start(f32[1024,1024]{1,0:T(8,128)} %fusion.2) | copy-start | bytes 12582916
  373.1 6.3 %slice-start = ((f32[2560]{0:T(1024)}), f32[512]{0:T(512)S(1)}, s32[]{:S(2)}) async-start(f32[2560]{0:T(1024)} %copy-done.4), calls=%async_computation.6 | async-start | bytes 4096 | tf_op jit(solution)/shard_map/slice | solution.py:111
Sparse Core Ops, SparseCore 0:
  44.8 101.8 reduce-scatter.3
  174.6 56.1 all-gather.1
  235.0 144.2 all-reduce.1

commit v4 on v3

--- a/solution.py
+++ b/solution.py
@@ -171,11 +171,13 @@
         diag = jnp.where(subject == column, ridge_part[None, :], jnp.zeros_like(kernel))
         return kernel + diag - update
 
-    head_gram, head_update = in_one_piece_2(
-        (gram_part[:leading], update_part[:leading]), "col", 1, 0)
+    head_part = jnp.concatenate([gram_part[:leading], update_part[:leading]], axis=0)
+    head_tiles = head_part.reshape(2 * leading, lanes, cols_here).transpose(1, 0, 2)
+    head_sum = lax.all_to_all(head_tiles, "col", 0, 0, tiled=True).sum(axis=0)
+    head_gram, head_update = head_sum[:leading], head_sum[leading:]
     head = system_of(head_gram, head_update, row_sq[:leading], 0)
     by_rows = subject_rows(gather_directly(head, "row", 0), groups, leading)
-    square = lax.all_gather(by_rows, "col", axis=1, tiled=True)
+    square = gather_directly(by_rows, "col", 1)
     gram_part, update_part, square = lax.optimization_barrier((gram_part, update_part, square))
     n = square.shape[0]
     i = lax.broadcasted_iota(jnp.int32, (n, n), 0)

time: 397 us -> 326 us (0.82)
  waiting for transfers between devices: 142 us -> 17.2 us
  blocking collectives: 55.6 us -> 107 us
    unnamed x4 -> x1, waiting for transfers between devices: 75.1 us -> 0.02 us
    all_gather x1 -> x0, waiting for transfers between devices: 56.2 us -> none  [body(): square = lax.all_gather(by_rows, 'col', axis=1, tiled=True)]
    all_to_all x1 -> x2, blocking collectives: 23.9 us -> 75.2 us  [copy_for_each(): lax.all_to_all(jnp.broadcast_to(x[None], (count, *x.shape)), axis, 0, 0,...]
    all_to_all x0 -> x1, waiting for transfers between devices: none -> 11.3 us  [body(): head_sum = lax.all_to_all(head_tiles, 'col', 0, 0, tiled=True).sum(axis=0)]
  transfers between devices with their start and end apart: 4 -> 3, of which waited for: 4 -> 2; matrix products, arithmetic and copies ran while one was open for 6% -> 7% of each run, Pallas kernels for 31% -> 38%
where the time goes in v4:
time: 326 us; the launch traced here: 320 us
  Pallas kernels  122 us (37%)
  blocking collectives  107 us (33%)
  starting transfers between devices  19 us (6%)
  local copies, waits for them, and re-layouts  18.5 us (6%)
  waiting for transfers between devices  17.2 us (5%)
  other arithmetic  15.9 us (5%)
  between operations  14.1 us (4%)
  matrix products  6.58 us (2%)
    pallas_call x1, Pallas kernels, chol_rows(): pl.pallas_call(_chol_rows_kernel, out_shape=jax.ShapeDtypeStruct(aug.shap...  122 us
    all_to_all x2, blocking collectives, copy_for_each(): lax.all_to_all(jnp.broadcast_to(x[None], (count, *x.shape)), axis, 0, 0,...  75.2 us
    all_gather x1, blocking collectives, in_one_piece(): whole = lax.all_gather(both, axis, axis=dim, tiled=True)  31.8 us
    all_to_all x1, starting transfers between devices, copy_for_each(): lax.all_to_all(jnp.broadcast_to(x[None], (count, *x.shape)), axis, 0, 0,...  15.3 us
    all_to_all x1, waiting for transfers between devices, body(): head_sum = lax.all_to_all(head_tiles, 'col', 0, 0, tiled=True).sum(axis=0)  11.3 us
  transfers between devices with their start and end apart: 3, of which 2 were waited for; matrix products, arithmetic and copies ran while one was open for 7% of the time, Pallas kernels for 38%

profile of v4, /device:TPU:1, one launch (start us, length us, event | category | flops | bytes accessed | tf_op | source)
XLA Modules:
  0.0 320.3 jit_solution(4313013462414710604)
XLA Ops:
  6.5 1.1 multiply_reduce_fusion.1
  7.7 0.7 slice.40
  8.4 0.7 slice.41
  9.2 31.8 %all_gather.3 = bf16[1024,192]{1,0:T(8,128)(2,1)S(1)} all-gather(bf16[64,192]{1,0:T(8,128)(2,1)S(1)} %pad_maximum_fusion.3), channel_id=1, replica_groups=mesh['row'=16,'col'=32] {'row'}, dimensions={0}, use_global_device_ids=true | all-gather | bytes 417792 | tf_op jit(solution)/shard_map/all_gather | solution.py:93
  41.4 0.8 dynamic_update_slice.3
  42.3 0.9 broadcast_in_dim.28
  43.2 15.3 %all-to-all-start = ((f32[32,1,2560]{2,1,0:T(1,128)}), f32[32,1,2560]{2,1,0:T(1,128)S(1)}, u32[]{:S(2)}, u32[]{:S(2)}) async-start(f32[32,1,2560]{2,1,0:T(1,128)} %broadcast_in_dim.28), calls=%async_computation | async-start | bytes 655360 | tf_op jit(solution)/shard_map/all_to_all | solution.py:99
  59.9 1.3 copy-done.1
  61.2 1.0 copy.41
  62.2 5.9 %all-to-all-done = f32[32,1,2560]{2,1,0:T(1,128)S(1)} async-done(((f32[32,1,2560]{2,1,0:T(1,128)}), f32[32,1,2560]{2,1,0:T(1,128)S(1)}, u32[]{:S(2)}, u32[]{:S(2)}) %all-to-all-start) | async-done | bytes 327712 | tf_op jit(solution)/shard_map/all_to_all | solution.py:99
  68.1 3.7 %all-to-all-start.1 = ((f32[32,128,32]{1,2,0:T(8,128)}), f32[32,128,32]{1,2,0:T(8,128)S(1)}, u32[]{:S(2)}, u32[]{:S(2)}) async-start(f32[32,128,32]{1,2,0:T(8,128)} %bitcast.10), calls=%async_computation.1 | async-start | bytes 1048576 | tf_op jit(solution)/shard_map/all_to_all | solution.py:176
  72.2 11.3 %all-to-all-done.1 = f32[32,128,32]{1,2,0:T(8,128)S(1)} async-done(((f32[32,128,32]{1,2,0:T(8,128)}), f32[32,128,32]{1,2,0:T(8,128)S(1)}, u32[]{:S(2)}, u32[]{:S(2)}) %all-to-all-start.1) | async-done | bytes 524320 | tf_op jit(solution)/shard_map/all_to_all | solution.py:176
  83.8 18.5 %all_to_all.21 = f32[16,1,2048]{2,1,0:T(1,128)S(1)} all-to-all(f32[16,1,2048]{2,1,0:T(1,128)S(1)} %reshape.39), channel_id=1, replica_groups=mesh['row'=16,'col'=32] {'row'}, dimensions={0} | all-to-all | bytes 262144 | tf_op jit(solution)/shard_map/all_to_all | solution.py:99
  102.4 0.6 broadcast.31
  103.0 1.0 reduce.2
  105.1 56.6 %all_to_all.22 = f32[32,1024,32]{1,2,0:T(8,128)} all-to-all(f32[32,1024,32]{1,2,0:T(8,128)S(1)} %broadcast_in_dim.56), channel_id=1, replica_groups=mesh['row'=16,'col'=32] {'col'}, dimensions={0} | all-to-all | bytes 8388608 | tf_op jit(solution)/shard_map/all_to_all | solution.py:99
  161.7 2.3 pad_maximum_fusion.1
  164.1 2.5 fusion.2
  166.5 5.4 %copy.44 = f32[1024,1024]{1,0:T(8,128)} copy(f32[1024,1024]{0,1:T(8,128)} %bitcast.38) | data formatting | bytes 8388608 | tf_op jit(solution)/shard_map/optimization_barrier | solution.py:181
  171.9 4.7 %fusion.1 = f32[1024,1024]{1,0:T(8,128)S(1)} fusion(f32[1024,1024]{1,0:T(8,128)} %copy.44, f32[1024,1024]{0,1:T(8,128)} %bitcast.39, pred[1024]{0:T(1024)(128)(4,1)S(1)} %iota_compare_fusion.4), kind=kLoop, calls=%fused_computation.5 | loop fusion | flops 6291456 | bytes 12583936 | tf_op jit(solution)/shard_map/jit(_where)/select_n | solution.py:187
  176.8 3.8 %pad_maximum_fusion.a_ref = f32[1024,2048]{1,0:T(8,128)} fusion(f32[1024,1024]{1,0:T(8,128)S(1)} %copy-done, f32[1024,1024]{1,0:T(8,128)S(1)} %fusion.1), kind=kLoop, calls=%fused_computation | loop fusion | flops 2097152 | bytes 16777216 | tf_op jit(solution)/shard_map/concatenate | solution.py:189
  180.6 122.0 %shard_map.37 = f32[1024,2048]{1,0:T(8,128)} custom-call(f32[1024,2048]{1,0:T(8,128)} %pad_maximum_fusion.a_ref), custom_call_target="tpu_custom_call" | custom-call | tf_op jit(solution)/shard_map/pallas_call | solution.py:81
  302.6 4.8 %slice.63 = f32[1024,1024]{1,0:T(8,128)} slice(f32[1024,2048]{1,0:T(8,128)} %shard_map.37), slice={[0:1024], [1024:2048]} | slice | bytes 8388608 | tf_op jit(solution)/shard_map/slice | solution.py:190
  307.4 5.7 %fusion.3 = f32[512,32]{0,1:T(8,128)} fusion(f32[1024,1024]{1,0:T(8,128)} %all-reduce.2.cloned.1.call-done, f32[1024]{0:T(1024)S(1)} %get-tuple-element.11, s32[512]{0:T(512)S(1)} %multiply_add_fusion, f32[1024]{0:T(1024)S(1)} %get-tuple-element.12, f32[512]{0:T(512)S(1)} %slice-done, f32[1024,1024]{1,0:T(8,128)} %slice.63, s32[]{:T(128)S(6)} %select_n.20), kind=kOutput, calls=%fused_computation.10 | convolution fusion | flops 206045184 | bytes 4403204 | tf_op jit(solution)/shard_map/dot_general | solution.py:195
  (51 shorter events, 3.9 us)
Async XLA Ops:
  6.5 52.3 %copy-start.3 = (bf16[512,128]{1,0:T(8,128)(2,1)S(1)}, bf16[512,128]{1,0:T(8,128)(2,1)}, u32[]{:S(2)}) copy-start(bf16[512,128]{1,0:T(8,128)(2,1)} %param.3) | copy-start | bytes 393220
  6.5 52.8 %copy-start.4 = (bf16[512,64]{0,1:T(8,128)(2,1)S(1)}, bf16[512,64]{0,1:T(8,128)(2,1)}, u32[]{:S(2)}) copy-start(bf16[512,64]{0,1:T(8,128)(2,1)} %param.4) | copy-start | bytes 196612
  43.2 24.9 %all-to-all-start = ((f32[32,1,2560]{2,1,0:T(1,128)}), f32[32,1,2560]{2,1,0:T(1,128)S(1)}, u32[]{:S(2)}, u32[]{:S(2)}) async-start(f32[32,1,2560]{2,1,0:T(1,128)} %broadcast_in_dim.28), calls=%async_computation | async-start | bytes 655360 | tf_op jit(solution)/shard_map/all_to_all | solution.py:99
  59.3 24.2 %copy-start.6 = (f32[32]{0:T(128)S(1)}, f32[32]{0:T(128)}, u32[]{:S(2)}) copy-start(f32[32]{0:T(128)} %param.5) | copy-start | bytes 388
  59.8 1.3 copy-start.1
  68.1 15.4 %all-to-all-start.1 = ((f32[32,128,32]{1,2,0:T(8,128)}), f32[32,128,32]{1,2,0:T(8,128)S(1)}, u32[]{:S(2)}, u32[]{:S(2)}) async-start(f32[32,128,32]{1,2,0:T(8,128)} %bitcast.10), calls=%async_computation.1 | async-start | bytes 1048576 | tf_op jit(solution)/shard_map/all_to_all | solution.py:176
  71.8 235.6 %all-reduce.2.cloned.1.call-start = ((), (), s32[]{:S(2)}) async-start(), calls=%async_computation.4 | async-start | bytes 8388608 | tf_op jit(solution)/shard_map/psum | solution.py:192
  72.1 94.5 %copy-start.5 = (f32[2560]{0:T(1024)}, f32[2560]{0:T(1024)S(1)}, u32[]{:S(2)}) copy-start(f32[2560]{0:T(1024)S(1)} %reduce_sum.41) | copy-start | bytes 30724
  105.1 56.6 %copy-start.2 = (f32[512,1024]{1,0:T(8,128)S(1)}, f32[512,1024]{1,0:T(8,128)}, u32[]{:S(2)}) copy-start(f32[512,1024]{1,0:T(8,128)} %copy-done.1) | copy-start | bytes 6291460
  171.9 4.9 %copy-start = (f32[1024,1024]{1,0:T(8,128)S(1)}, f32[1024,1024]{1,0:T(8,128)}, u32[]{:S(2)}) copy-start(f32[1024,1024]{1,0:T(8,128)} %fusion.2) | copy-start | bytes 12582916
  302.6 4.8 %slice-start = ((f32[2560]{0:T(1024)}), f32[512]{0:T(512)S(1)}, s32[]{:S(2)}) async-start(f32[2560]{0:T(1024)} %copy-done.5), calls=%async_computation.5 | async-start | bytes 4096 | tf_op jit(solution)/shard_map/slice | solution.py:111
Sparse Core Ops, SparseCore 0:
  164.2 135.0 all-reduce.1

commit v5 on v4

--- a/solution.py
+++ b/solution.py
@@ -187,7 +187,7 @@
     sym = jnp.where(same, (square + flipped) * 0.5, jnp.where(i < j, flipped, square))
     eye = (i == j).astype(jnp.float32)
     done = chol_rows(jnp.concatenate([sym, eye], axis=1))
-    inv_t = lax.dynamic_slice_in_dim(done[:, n:], col_start, cols_here, 0)
+    inv_t = lax.dynamic_slice(done, (col_start, n), (cols_here, n))
 
     both = lax.psum(jnp.concatenate([gram_part, update_part], axis=0), "col")
     gram, update = both[:rows_here], both[rows_here:]

time: 326 us -> 322 us (0.988)
  local copies, waits for them, and re-layouts: 18.5 us -> 13.8 us
    slice x1 -> x0, local copies, waits for them, and re-layouts: 4.76 us -> none  [body(): inv_t = lax.dynamic_slice_in_dim(done[:, n:], col_start, cols_here, 0)]
  transfers between devices with their start and end apart: 3 -> 3, of which waited for: 2 -> 2; matrix products, arithmetic and copies ran while one was open for 7% -> 6% of each run, Pallas kernels for 38% -> 39%
where the time goes in v5:
time: 322 us; the launch traced here: 316 us
  Pallas kernels  122 us (38%)
  blocking collectives  107 us (33%)
  starting transfers between devices  19 us (6%)
  waiting for transfers between devices  17.2 us (5%)
  other arithmetic  15.9 us (5%)
  between operations  14.1 us (4%)
  local copies, waits for them, and re-layouts  13.8 us (4%)
  matrix products  6.58 us (2%)
    pallas_call x1, Pallas kernels, chol_rows(): pl.pallas_call(_chol_rows_kernel, out_shape=jax.ShapeDtypeStruct(aug.shap...  122 us
    all_to_all x2, blocking collectives, copy_for_each(): lax.all_to_all(jnp.broadcast_to(x[None], (count, *x.shape)), axis, 0, 0,...  75.2 us
    all_gather x1, blocking collectives, in_one_piece(): whole = lax.all_gather(both, axis, axis=dim, tiled=True)  31.8 us
    all_to_all x1, starting transfers between devices, copy_for_each(): lax.all_to_all(jnp.broadcast_to(x[None], (count, *x.shape)), axis, 0, 0,...  15.3 us
    all_to_all x1, waiting for transfers between devices, body(): head_sum = lax.all_to_all(head_tiles, 'col', 0, 0, tiled=True).sum(axis=0)  11.3 us
  transfers between devices with their start and end apart: 3, of which 2 were waited for; matrix products, arithmetic and copies ran while one was open for 6% of the time, Pallas kernels for 39%

profile of v5, /device:TPU:1, one launch (start us, length us, event | category | flops | bytes accessed | tf_op | source)
XLA Modules:
  0.0 315.6 jit_solution(2979850220436208645)
XLA Ops:
  6.5 1.1 multiply_reduce_fusion.1
  7.7 0.7 slice.37
  8.4 0.7 slice.38
  9.2 31.8 %all_gather.3 = bf16[1024,192]{1,0:T(8,128)(2,1)S(1)} all-gather(bf16[64,192]{1,0:T(8,128)(2,1)S(1)} %pad_maximum_fusion.3), channel_id=1, replica_groups=mesh['row'=16,'col'=32] {'row'}, dimensions={0}, use_global_device_ids=true | all-gather | bytes 417792 | tf_op jit(solution)/shard_map/all_gather | solution.py:93
  41.4 0.8 dynamic_update_slice.3
  42.3 0.9 broadcast_in_dim.28
  43.2 15.3 %all-to-all-start = ((f32[32,1,2560]{2,1,0:T(1,128)}), f32[32,1,2560]{2,1,0:T(1,128)S(1)}, u32[]{:S(2)}, u32[]{:S(2)}) async-start(f32[32,1,2560]{2,1,0:T(1,128)} %broadcast_in_dim.28), calls=%async_computation | async-start | bytes 655360 | tf_op jit(solution)/shard_map/all_to_all | solution.py:99
  59.9 1.3 copy-done.1
  61.2 1.0 copy.41
  62.2 5.9 %all-to-all-done = f32[32,1,2560]{2,1,0:T(1,128)S(1)} async-done(((f32[32,1,2560]{2,1,0:T(1,128)}), f32[32,1,2560]{2,1,0:T(1,128)S(1)}, u32[]{:S(2)}, u32[]{:S(2)}) %all-to-all-start) | async-done | bytes 327712 | tf_op jit(solution)/shard_map/all_to_all | solution.py:99
  68.1 3.7 %all-to-all-start.1 = ((f32[32,128,32]{1,2,0:T(8,128)}), f32[32,128,32]{1,2,0:T(8,128)S(1)}, u32[]{:S(2)}, u32[]{:S(2)}) async-start(f32[32,128,32]{1,2,0:T(8,128)} %bitcast.10), calls=%async_computation.1 | async-start | bytes 1048576 | tf_op jit(solution)/shard_map/all_to_all | solution.py:176
  72.2 11.3 %all-to-all-done.1 = f32[32,128,32]{1,2,0:T(8,128)S(1)} async-done(((f32[32,128,32]{1,2,0:T(8,128)}), f32[32,128,32]{1,2,0:T(8,128)S(1)}, u32[]{:S(2)}, u32[]{:S(2)}) %all-to-all-start.1) | async-done | bytes 524320 | tf_op jit(solution)/shard_map/all_to_all | solution.py:176
  83.8 18.5 %all_to_all.21 = f32[16,1,2048]{2,1,0:T(1,128)S(1)} all-to-all(f32[16,1,2048]{2,1,0:T(1,128)S(1)} %reshape.39), channel_id=1, replica_groups=mesh['row'=16,'col'=32] {'row'}, dimensions={0} | all-to-all | bytes 262144 | tf_op jit(solution)/shard_map/all_to_all | solution.py:99
  102.4 0.6 broadcast.31
  103.0 1.0 reduce.2
  104.6 0.5 broadcast_in_dim.56
  105.1 56.6 %all_to_all.22 = f32[32,1024,32]{1,2,0:T(8,128)} all-to-all(f32[32,1024,32]{1,2,0:T(8,128)S(1)} %broadcast_in_dim.56), channel_id=1, replica_groups=mesh['row'=16,'col'=32] {'col'}, dimensions={0} | all-to-all | bytes 8388608 | tf_op jit(solution)/shard_map/all_to_all | solution.py:99
  161.7 2.3 pad_maximum_fusion.1
  164.1 2.5 fusion.2
  166.5 5.4 %copy.44 = f32[1024,1024]{1,0:T(8,128)} copy(f32[1024,1024]{0,1:T(8,128)} %bitcast.38) | data formatting | bytes 8388608 | tf_op jit(solution)/shard_map/optimization_barrier | solution.py:181
  171.9 4.7 %fusion.1 = f32[1024,1024]{1,0:T(8,128)S(1)} fusion(f32[1024,1024]{1,0:T(8,128)} %copy.44, f32[1024,1024]{0,1:T(8,128)} %bitcast.39, pred[1024]{0:T(1024)(128)(4,1)S(1)} %iota_compare_fusion.4), kind=kLoop, calls=%fused_computation.5 | loop fusion | flops 6291456 | bytes 12583936 | tf_op jit(solution)/shard_map/jit(_where)/select_n | solution.py:187
  176.8 3.8 %pad_maximum_fusion.a_ref = f32[1024,2048]{1,0:T(8,128)} fusion(f32[1024,1024]{1,0:T(8,128)S(1)} %copy-done, f32[1024,1024]{1,0:T(8,128)S(1)} %fusion.1), kind=kLoop, calls=%fused_computation | loop fusion | flops 2097152 | bytes 16777216 | tf_op jit(solution)/shard_map/concatenate | solution.py:189
  180.6 122.0 %shard_map.37 = f32[1024,2048]{1,0:T(8,128)} custom-call(f32[1024,2048]{1,0:T(8,128)} %pad_maximum_fusion.a_ref), custom_call_target="tpu_custom_call" | custom-call | tf_op jit(solution)/shard_map/pallas_call | solution.py:81
  302.6 5.7 %fusion.3 = f32[512,32]{0,1:T(8,128)} fusion(f32[1024,1024]{1,0:T(8,128)} %all-reduce.2.cloned.1.call-done, f32[1024]{0:T(1024)S(1)} %get-tuple-element.11, s32[512]{0:T(512)S(1)} %multiply_add_fusion, f32[1024]{0:T(1024)S(1)} %get-tuple-element.12, f32[512]{0:T(512)S(1)} %slice-done, f32[1024,2048]{1,0:T(8,128)} %shard_map.37, s32[]{:T(128)S(6)} %select_n.20), kind=kOutput, calls=%fused_computation.10 | convolution fusion | flops 206045184 | bytes 4403204 | tf_op jit(solution)/shard_map/dot_general | solution.py:195
  (50 shorter events, 3.3 us)
Async XLA Ops:
  6.5 52.3 %copy-start.3 = (bf16[512,128]{1,0:T(8,128)(2,1)S(1)}, bf16[512,128]{1,0:T(8,128)(2,1)}, u32[]{:S(2)}) copy-start(bf16[512,128]{1,0:T(8,128)(2,1)} %param.3) | copy-start | bytes 393220
  6.5 52.8 %copy-start.4 = (bf16[512,64]{0,1:T(8,128)(2,1)S(1)}, bf16[512,64]{0,1:T(8,128)(2,1)}, u32[]{:S(2)}) copy-start(bf16[512,64]{0,1:T(8,128)(2,1)} %param.4) | copy-start | bytes 196612
  43.2 24.9 %all-to-all-start = ((f32[32,1,2560]{2,1,0:T(1,128)}), f32[32,1,2560]{2,1,0:T(1,128)S(1)}, u32[]{:S(2)}, u32[]{:S(2)}) async-start(f32[32,1,2560]{2,1,0:T(1,128)} %broadcast_in_dim.28), calls=%async_computation | async-start | bytes 655360 | tf_op jit(solution)/shard_map/all_to_all | solution.py:99
  59.3 24.2 %copy-start.6 = (f32[32]{0:T(128)S(1)}, f32[32]{0:T(128)}, u32[]{:S(2)}) copy-start(f32[32]{0:T(128)} %param.5) | copy-start | bytes 388
  59.8 1.3 copy-start.1
  68.1 15.4 %all-to-all-start.1 = ((f32[32,128,32]{1,2,0:T(8,128)}), f32[32,128,32]{1,2,0:T(8,128)S(1)}, u32[]{:S(2)}, u32[]{:S(2)}) async-start(f32[32,128,32]{1,2,0:T(8,128)} %bitcast.10), calls=%async_computation.1 | async-start | bytes 1048576 | tf_op jit(solution)/shard_map/all_to_all | solution.py:176
  71.8 230.8 %all-reduce.2.cloned.1.call-start = ((), (), s32[]{:S(2)}) async-start(), calls=%async_computation.4 | async-start | bytes 8388608 | tf_op jit(solution)/shard_map/psum | solution.py:192
  72.1 94.5 %copy-start.5 = (f32[2560]{0:T(1024)}, f32[2560]{0:T(1024)S(1)}, u32[]{:S(2)}) copy-start(f32[2560]{0:T(1024)S(1)} %reduce_sum.41) | copy-start | bytes 30724
  105.1 56.6 %copy-start.2 = (f32[512,1024]{1,0:T(8,128)S(1)}, f32[512,1024]{1,0:T(8,128)}, u32[]{:S(2)}) copy-start(f32[512,1024]{1,0:T(8,128)} %copy-done.1) | copy-start | bytes 6291460
  171.9 4.9 %copy-start = (f32[1024,1024]{1,0:T(8,128)S(1)}, f32[1024,1024]{1,0:T(8,128)}, u32[]{:S(2)}) copy-start(f32[1024,1024]{1,0:T(8,128)} %fusion.2) | copy-start | bytes 12582916
  180.6 122.1 %slice-start = ((f32[2560]{0:T(1024)}), f32[512]{0:T(512)S(1)}, s32[]{:S(2)}) async-start(f32[2560]{0:T(1024)} %copy-done.5), calls=%async_computation.5 | async-start | bytes 4096 | tf_op jit(solution)/shard_map/slice | solution.py:111
Sparse Core Ops, SparseCore 0:
  164.2 135.0 all-reduce.1
